TPU v7x, 128 devices: a whole 4x4x4 slice. The times are simulated.
128 devices in a mesh: outer: 16 (over z_hi, y, core), inner: 8 (over x, z_lo).
Axes of the slice: x: 4, y: 4, z: 4 (z_hi: 2, z_lo: 2; z = z_hi * 2 + z_lo), core: 2. Of those that a mesh axis runs over, the one named last changes fastest.
Arguments:
- q_load: bfloat16 [131072, 512], P(('outer', 'inner')), may hold values from -8 to 8
- kv_load: bfloat16 [131072, 256], P(('outer', 'inner')), may hold values from -8 to 8
- pack_dest: int32 [128, 8], P('outer'), may hold values from -1 to 31, as said below
- counts: int32 [128], P('outer'), may hold values from 0 to 8, as said below
- segment_ids: int32 [65536], P(('outer', 'inner')), may hold values from 0 to 7, never falling along the last dimension, each value on 1 to 16384 neighbouring positions
Outputs:
- attn_out: bfloat16 [65536, 512], P(('outer', 'inner'))
Inputs may be any that keep to these rules, and one draw needn't show every extreme that they name: In each group of 8 loader shards that share an outer index the counts add up to 32; some shard of every group holds 8 live blocks and some holds none. `pack_dest`: live entries of a group name every block number 0 to 31 exactly once; block number t goes to the device of inner index t // 4 in the same group, as its block t % 4; a shard sends at most 1 block to one device, and some shard sends exactly 1; entries of slots that are not live are -1. `segment_ids`: never falling along the sequence.
All inputs are finite; a program needn't handle non-finite values.
Results may differ from a plain program's by a relative error of at most 0.0059.
Values may be sent and summed in bfloat16 or wider, within the bound.
No kernel may reach another device: no remote copies, remote signals or barrier semaphores. Data moves between devices by JAX's collectives and lax.ppermute only.
A program may use at most 64 MiB of HBM per device.

v0:
```python
import math

import jax
import jax.numpy as jnp
from jax import lax
from jax.sharding import PartitionSpec as P


def shifted(value, axis, steps):
    count = lax.axis_size(axis)
    leading, last = (max(0, -steps), min(count, count - steps))
    return lax.ppermute(value, axis, [(source, source + steps) for source in range(leading, last)])


def select_rows(selector, blocks, pattern):
    return jnp.einsum(
        pattern, selector.astype(jnp.bfloat16), blocks, preferred_element_type=jnp.float32
    ).astype(jnp.bfloat16)


def local(q_load, kv_load, pack_dest, counts, segment_ids):
    group_width = lax.axis_size("inner")
    my_index = lax.axis_index("inner")
    capacity = pack_dest.shape[1]
    slot_count = capacity // 2
    pair_limit = -(-capacity // group_width)
    row_length = q_load.shape[0] // capacity
    query_width = q_load.shape[1]
    pair_width = kv_load.shape[1]
    head_size = pair_width // 2
    head_count = query_width // head_size
    slot_grid = lax.broadcasted_iota(jnp.int32, (group_width, capacity), 1)
    live_all = slot_grid < counts[:, None]
    owner_all = pack_dest // slot_count
    slot_numbers = jnp.arange(capacity, dtype=jnp.int32)
    earlier = slot_numbers[None, :] < slot_numbers[:, None]
    same_owner = owner_all[:, :, None] == owner_all[:, None, :]
    rank_all = jnp.sum(
        (earlier[None] & same_owner & live_all[:, None, :]).astype(jnp.int32), axis=2
    )
    shard_rows = jnp.arange(group_width, dtype=jnp.int32)
    mine_row = (shard_rows == my_index)[:, None]
    my_owner = jnp.sum(jnp.where(mine_row, owner_all, 0), axis=0)
    my_rank = jnp.sum(jnp.where(mine_row, rank_all, 0), axis=0)
    my_live = jnp.any(mine_row & live_all, axis=0)
    pair_ids = jnp.arange(pair_limit, dtype=jnp.int32)
    send_select = (
        my_live[None, None, :]
        & (my_owner[None, None, :] == shard_rows[:, None, None])
        & (my_rank[None, None, :] == pair_ids[None, :, None])
    )
    q_blocks = q_load.reshape(capacity, row_length, query_width)
    kv_blocks = kv_load.reshape(capacity, row_length, pair_width)
    send_q = select_rows(send_select, q_blocks, "jkc,crf->jkrf")
    send_kv = select_rows(send_select, kv_blocks, "jkc,crf->jkrf")
    recv_q, recv_kv = (
        lax.all_to_all(send_q, "inner", split_axis=0, concat_axis=0, tiled=True),
        lax.all_to_all(send_kv, "inner", split_axis=0, concat_axis=0, tiled=True),
    )
    wanted = my_index * slot_count + jnp.arange(slot_count, dtype=jnp.int32)
    take_select = jnp.any(
        live_all[None, :, None, :]
        & (pack_dest[None, :, None, :] == wanted[:, None, None, None])
        & (rank_all[None, :, None, :] == pair_ids[None, None, :, None]),
        axis=3,
    )
    q_seq = select_rows(take_select, recv_q, "srk,rktf->stf").reshape(
        slot_count * row_length, query_width
    )
    kv_seq = select_rows(take_select, recv_kv, "srk,rktf->stf").reshape(
        slot_count * row_length, pair_width
    )
    tok_rows = q_seq.shape[0]
    owner_index = lax.axis_index(("outer", "inner"))
    query_pos = owner_index * tok_rows + jnp.arange(tok_rows, dtype=jnp.int32)
    queries = q_seq.reshape(tok_rows, head_count, head_size)
    score_scale = 1.0 / math.sqrt(head_size)
    last_pos = query_pos[tok_rows - 1]
    first_seg = segment_ids[0]
    last_seg = segment_ids[tok_rows - 1]

    def update(running, key_rows, key_seg, key_pos):
        largest, denominator, weighted = running
        key_part = key_rows[:, :head_size]
        value_part = key_rows[:, head_size:]
        scores = (
            jnp.einsum("qhd,kd->hqk", queries, key_part, preferred_element_type=jnp.float32)
            * score_scale
        )
        visible = (
            (key_pos[None, :] >= 0)
            & (key_pos[None, :] <= query_pos[:, None])
            & (key_seg[None, :] == segment_ids[:, None])
        )
        masked = jnp.where(visible[None], scores, -1e30)
        newest = jnp.maximum(largest, jnp.max(masked, axis=-1))
        factor = jnp.exp(largest - newest)
        weights = jnp.where(visible[None], jnp.exp(masked - newest[:, :, None]), 0.0)
        denominator = denominator * factor + jnp.sum(weights, axis=-1)
        weighted = weighted * factor.T[:, :, None] + jnp.einsum(
            "hqk,kd->qhd",
            weights.astype(jnp.bfloat16),
            value_part,
            preferred_element_type=jnp.float32,
        )
        return (newest, denominator, weighted)

    def absorb(running, pieces, first_row):
        key_rows, key_seg = pieces
        row_total = key_rows.shape[0]
        block_rows = 512

        def one_block(block_index, state):
            offset = block_index * block_rows
            rows_now = key_rows
            seg_now = key_seg
            pos_now = first_row + offset + jnp.arange(block_rows, dtype=jnp.int32)

            def compute(inner_state):
                return update(inner_state, rows_now, seg_now, pos_now)

            def keep(inner_state):
                return inner_state

            needed = (
                (pos_now[0] <= last_pos)
                & (seg_now[block_rows - 1] >= first_seg)
                & (seg_now[0] <= last_seg)
            )
            return lax.cond(needed, compute, keep, state)

        return lax.fori_loop(0, row_total // block_rows, one_block, running)

    initial = (
        jnp.full((head_count, tok_rows), -1e30, jnp.float32),
        jnp.zeros((head_count, tok_rows), jnp.float32),
        jnp.zeros((tok_rows, head_count, head_size), jnp.float32),
    )
    device_reach = lax.axis_size("outer") * group_width // 4
    own_state = absorb(initial, (kv_seq, segment_ids), owner_index * tok_rows)

    def travel(step, carry):
        state, rows_now, seg_now = carry
        rows_now, seg_now = shifted((rows_now, seg_now), ("outer", "inner"), 1)
        state = absorb(state, (rows_now, seg_now), (owner_index - step - 1) * tok_rows)
        return (state, rows_now, seg_now)

    result = lax.fori_loop(0, device_reach, travel, (own_state, kv_seq, segment_ids))[0]
    largest, denominator, weighted = result
    return (
        (weighted / denominator.T[:, :, None]).reshape(tok_rows, query_width).astype(jnp.bfloat16)
    )


def solution(mesh):
    in_specs = (
        P(("outer", "inner"), None),
        P(("outer", "inner"), None),
        P("outer", None),
        P("outer"),
        P(("outer", "inner")),
    )
    out_specs = P(("outer", "inner"), None)
    return jax.shard_map(local, mesh=mesh, in_specs=in_specs, out_specs=out_specs, check_vma=False)
```

profile of v0, /device:TPU:74, one launch (start us, length us, event | category | flops | bytes accessed | tf_op | source)
XLA Modules:
  0.0 637.5 jit_solution(16620829819080739277)
XLA Ops:
  4.9 6.0 all-to-all-start
  19.1 5.5 all-to-all-start.1
  27.3 10.8 %all-to-all-done.1 = bf16[8,1,128,512]{3,2,1,0:T(8,128)(2,1)} async-done(((bf16[8,1,128,512]{3,2,1,0:T(8,128)(2,1)}), bf16[8,1,128,512]{3,2,1,0:T(8,128)(2,1)}, u32[]{:S(2)}, u32[]{:S(2)}) %all-to-all-start.1) | async-done | bytes 1048608 | tf_op jit(solution)/shard_map/all_to_all | solution.py:57
  42.2 4.5 conditional.2
  46.6 589.8 %while.46 = (s32[]{:T(128)}, f32[4,512]{1,0:T(4,128)S(1)}, f32[4,512]{1,0:T(4,128)S(1)}, f32[512,4,128]{2,0,1:T(8,128)S(1)}, bf16[512,256]{1,0:T(8,128)(2,1)S(1)...) while((s32[]{:T(128)}, f32[4,512]{1,0:T(4,128)S(1)}, ...), condition=%wide.region_14.15_spmd.clone, body=%wide.region_9.14_spmd.clone.sunk | while | flops 552082944 | bytes 18251224 | solution.py:148
  59.3 4.3 conditional.5
  76.1 4.3 conditional.5
  82.4 4.1 collective-permute-start
  92.9 4.3 conditional.5
  102.9 4.0 collective-permute-done
  110.1 4.3 conditional.5
  121.4 5.2 collective-permute-done
  129.9 4.3 conditional.5
  139.9 5.0 collective-permute-done
  148.2 4.3 conditional.5
  158.2 5.1 collective-permute-done
  166.5 4.3 conditional.5
  176.5 5.1 collective-permute-done
  184.9 4.3 conditional.5
  194.9 5.1 collective-permute-done
  203.2 4.3 conditional.5
  213.2 9.8 %collective-permute-done = s32[512]{0:T(512)S(1)} collective-permute-done((s32[512]{0:T(512)S(1)}, s32[512]{0:T(512)S(1)}, u32[]{:S(2)}, u32[]{:S(2)}) %collective-permute-start) | collective-permute-done | bytes 2080 | tf_op jit(solution)/shard_map/while/body/eval_jaxpr/ppermute | solution.py:12
  226.2 4.3 conditional.5
  236.2 3.6 collective-permute-done
  243.1 4.3 conditional.5
  253.1 4.5 collective-permute-done
  260.8 4.3 conditional.5
  270.8 8.2 %collective-permute-done = s32[512]{0:T(512)S(1)} collective-permute-done((s32[512]{0:T(512)S(1)}, s32[512]{0:T(512)S(1)}, u32[]{:S(2)}, u32[]{:S(2)}) %collective-permute-start) | collective-permute-done | bytes 2080 | tf_op jit(solution)/shard_map/while/body/eval_jaxpr/ppermute | solution.py:12
  282.3 4.3 conditional.5
  292.3 4.8 collective-permute-done
  300.3 4.3 conditional.5
  310.3 5.1 collective-permute-done
  318.7 4.3 conditional.5
  328.7 6.8 %collective-permute-done = s32[512]{0:T(512)S(1)} collective-permute-done((s32[512]{0:T(512)S(1)}, s32[512]{0:T(512)S(1)}, u32[]{:S(2)}, u32[]{:S(2)}) %collective-permute-start) | collective-permute-done | bytes 2080 | tf_op jit(solution)/shard_map/while/body/eval_jaxpr/ppermute | solution.py:12
  338.7 4.3 conditional.5
  348.7 4.7 collective-permute-done
  356.7 4.3 conditional.5
  366.7 3.7 collective-permute-done
  373.7 4.3 conditional.5
  383.7 7.8 %collective-permute-done = s32[512]{0:T(512)S(1)} collective-permute-done((s32[512]{0:T(512)S(1)}, s32[512]{0:T(512)S(1)}, u32[]{:S(2)}, u32[]{:S(2)}) %collective-permute-start) | collective-permute-done | bytes 2080 | tf_op jit(solution)/shard_map/while/body/eval_jaxpr/ppermute | solution.py:12
  394.8 4.3 conditional.5
  404.8 5.8 collective-permute-done
  413.9 4.3 conditional.5
  423.9 6.1 collective-permute-done
  433.3 4.3 conditional.5
  443.3 5.0 collective-permute-done
  451.6 4.3 conditional.5
  461.6 6.0 collective-permute-done
  470.9 4.3 conditional.5
  487.7 4.3 conditional.5
  497.7 3.6 collective-permute-done
  504.5 4.3 conditional.5
  521.3 4.3 conditional.5
  531.3 4.9 collective-permute-done
  539.5 4.3 conditional.5
  549.5 5.5 collective-permute-done
  558.3 4.3 conditional.5
  568.3 7.2 %collective-permute-done = s32[512]{0:T(512)S(1)} collective-permute-done((s32[512]{0:T(512)S(1)}, s32[512]{0:T(512)S(1)}, u32[]{:S(2)}, u32[]{:S(2)}) %collective-permute-start) | collective-permute-done | bytes 2080 | tf_op jit(solution)/shard_map/while/body/eval_jaxpr/ppermute | solution.py:12
  578.7 4.3 conditional.5
  595.5 4.3 conditional.5
  605.5 5.0 collective-permute-done
  613.7 4.3 conditional.5
  623.7 5.1 collective-permute-done
  632.1 4.3 conditional.5
  (623 shorter events, 336.5 us)
Async XLA Ops:
  4.9 14.1 %all-to-all-start = ((bf16[8,1,128,256]{3,2,1,0:T(8,128)(2,1)}), bf16[8,1,128,256]{3,2,1,0:T(8,128)(2,1)S(1)}, u32[]{:S(2)}, u32[]{:S(2)}) async-start(bf16[8,1,128,256]{3,2,1,0:T(8,128)(2,1)} %copy.36), calls=%async_computation | async-start | bytes 1048576 | tf_op jit(solution)/shard_map/all_to_all | solution.py:58
  19.1 19.0 %all-to-all-start.1 = ((bf16[8,1,128,512]{3,2,1,0:T(8,128)(2,1)}), bf16[8,1,128,512]{3,2,1,0:T(8,128)(2,1)}, u32[]{:S(2)}, u32[]{:S(2)}) async-start(bf16[8,1,128,512]{3,2,1,0:T(8,128)(2,1)} %copy.40), calls=%async_computation.1 | async-start | bytes 2097152 | tf_op jit(solution)/shard_map/all_to_all | solution.py:57
  46.7 12.6 %collective-permute-start.1 = (bf16[512,256]{1,0:T(8,128)(2,1)S(1)}, bf16[512,256]{1,0:T(8,128)(2,1)S(1)}, u32[]{:S(2)}, u32[]{:S(2)}) collective-permute-start(bf16[512,256]{1,0:T(8,128)(2,1)S(1)} %get-tuple-element.771), channel_id=1, source_target_pairs={{0,1},{1,2},{2,3},{3,4},{4,5},{5,6},{6,7},{7,8},{8,9},{9,10},{10,1... | collective-permute-start | bytes 786440 | tf_op jit(solution)/shard_map/while/body/eval_jaxpr/ppermute | solution.py:12
  63.7 12.4 %collective-permute-start.1 = (bf16[512,256]{1,0:T(8,128)(2,1)S(1)}, bf16[512,256]{1,0:T(8,128)(2,1)S(1)}, u32[]{:S(2)}, u32[]{:S(2)}) collective-permute-start(bf16[512,256]{1,0:T(8,128)(2,1)S(1)} %get-tuple-element.771), channel_id=1, source_target_pairs={{0,1},{1,2},{2,3},{3,4},{4,5},{5,6},{6,7},{7,8},{8,9},{9,10},{10,1... | collective-permute-start | bytes 786440 | tf_op jit(solution)/shard_map/while/body/eval_jaxpr/ppermute | solution.py:12
  65.6 7.3 %collective-permute-start = (s32[512]{0:T(512)S(1)}, s32[512]{0:T(512)S(1)}, u32[]{:S(2)}, u32[]{:S(2)}) collective-permute-start(s32[512]{0:T(512)S(1)} %get-tuple-element.772), channel_id=1, source_target_pairs={{0,1},{1,2},{2,3},{3,4},{4,5},{5,6},{6,7},{7,8},{8,9},{9,10},{10,1... | collective-permute-start | bytes 6152 | tf_op jit(solution)/shard_map/while/body/eval_jaxpr/ppermute | solution.py:12
  80.5 12.4 %collective-permute-start.1 = (bf16[512,256]{1,0:T(8,128)(2,1)S(1)}, bf16[512,256]{1,0:T(8,128)(2,1)S(1)}, u32[]{:S(2)}, u32[]{:S(2)}) collective-permute-start(bf16[512,256]{1,0:T(8,128)(2,1)S(1)} %get-tuple-element.771), channel_id=1, source_target_pairs={{0,1},{1,2},{2,3},{3,4},{4,5},{5,6},{6,7},{7,8},{8,9},{9,10},{10,1... | collective-permute-start | bytes 786440 | tf_op jit(solution)/shard_map/while/body/eval_jaxpr/ppermute | solution.py:12
  82.4 7.3 %collective-permute-start = (s32[512]{0:T(512)S(1)}, s32[512]{0:T(512)S(1)}, u32[]{:S(2)}, u32[]{:S(2)}) collective-permute-start(s32[512]{0:T(512)S(1)} %get-tuple-element.772), channel_id=1, source_target_pairs={{0,1},{1,2},{2,3},{3,4},{4,5},{5,6},{6,7},{7,8},{8,9},{9,10},{10,1... | collective-permute-start | bytes 6152 | tf_op jit(solution)/shard_map/while/body/eval_jaxpr/ppermute | solution.py:12
  97.3 12.9 %collective-permute-start.1 = (bf16[512,256]{1,0:T(8,128)(2,1)S(1)}, bf16[512,256]{1,0:T(8,128)(2,1)S(1)}, u32[]{:S(2)}, u32[]{:S(2)}) collective-permute-start(bf16[512,256]{1,0:T(8,128)(2,1)S(1)} %get-tuple-element.771), channel_id=1, source_target_pairs={{0,1},{1,2},{2,3},{3,4},{4,5},{5,6},{6,7},{7,8},{8,9},{9,10},{10,1... | collective-permute-start | bytes 786440 | tf_op jit(solution)/shard_map/while/body/eval_jaxpr/ppermute | solution.py:12
  99.2 7.7 %collective-permute-start = (s32[512]{0:T(512)S(1)}, s32[512]{0:T(512)S(1)}, u32[]{:S(2)}, u32[]{:S(2)}) collective-permute-start(s32[512]{0:T(512)S(1)} %get-tuple-element.772), channel_id=1, source_target_pairs={{0,1},{1,2},{2,3},{3,4},{4,5},{5,6},{6,7},{7,8},{8,9},{9,10},{10,1... | collective-permute-start | bytes 6152 | tf_op jit(solution)/shard_map/while/body/eval_jaxpr/ppermute | solution.py:12
  114.5 15.4 %collective-permute-start.1 = (bf16[512,256]{1,0:T(8,128)(2,1)S(1)}, bf16[512,256]{1,0:T(8,128)(2,1)S(1)}, u32[]{:S(2)}, u32[]{:S(2)}) collective-permute-start(bf16[512,256]{1,0:T(8,128)(2,1)S(1)} %get-tuple-element.771), channel_id=1, source_target_pairs={{0,1},{1,2},{2,3},{3,4},{4,5},{5,6},{6,7},{7,8},{8,9},{9,10},{10,1... | collective-permute-start | bytes 786440 | tf_op jit(solution)/shard_map/while/body/eval_jaxpr/ppermute | solution.py:12
  116.4 10.2 %collective-permute-start = (s32[512]{0:T(512)S(1)}, s32[512]{0:T(512)S(1)}, u32[]{:S(2)}, u32[]{:S(2)}) collective-permute-start(s32[512]{0:T(512)S(1)} %get-tuple-element.772), channel_id=1, source_target_pairs={{0,1},{1,2},{2,3},{3,4},{4,5},{5,6},{6,7},{7,8},{8,9},{9,10},{10,1... | collective-permute-start | bytes 6152 | tf_op jit(solution)/shard_map/while/body/eval_jaxpr/ppermute | solution.py:12
  134.2 13.9 %collective-permute-start.1 = (bf16[512,256]{1,0:T(8,128)(2,1)S(1)}, bf16[512,256]{1,0:T(8,128)(2,1)S(1)}, u32[]{:S(2)}, u32[]{:S(2)}) collective-permute-start(bf16[512,256]{1,0:T(8,128)(2,1)S(1)} %get-tuple-element.771), channel_id=1, source_target_pairs={{0,1},{1,2},{2,3},{3,4},{4,5},{5,6},{6,7},{7,8},{8,9},{9,10},{10,1... | collective-permute-start | bytes 786440 | tf_op jit(solution)/shard_map/while/body/eval_jaxpr/ppermute | solution.py:12
  136.2 8.8 %collective-permute-start = (s32[512]{0:T(512)S(1)}, s32[512]{0:T(512)S(1)}, u32[]{:S(2)}, u32[]{:S(2)}) collective-permute-start(s32[512]{0:T(512)S(1)} %get-tuple-element.772), channel_id=1, source_target_pairs={{0,1},{1,2},{2,3},{3,4},{4,5},{5,6},{6,7},{7,8},{8,9},{9,10},{10,1... | collective-permute-start | bytes 6152 | tf_op jit(solution)/shard_map/while/body/eval_jaxpr/ppermute | solution.py:12
  152.5 14.0 %collective-permute-start.1 = (bf16[512,256]{1,0:T(8,128)(2,1)S(1)}, bf16[512,256]{1,0:T(8,128)(2,1)S(1)}, u32[]{:S(2)}, u32[]{:S(2)}) collective-permute-start(bf16[512,256]{1,0:T(8,128)(2,1)S(1)} %get-tuple-element.771), channel_id=1, source_target_pairs={{0,1},{1,2},{2,3},{3,4},{4,5},{5,6},{6,7},{7,8},{8,9},{9,10},{10,1... | collective-permute-start | bytes 786440 | tf_op jit(solution)/shard_map/while/body/eval_jaxpr/ppermute | solution.py:12
  154.5 8.8 %collective-permute-start = (s32[512]{0:T(512)S(1)}, s32[512]{0:T(512)S(1)}, u32[]{:S(2)}, u32[]{:S(2)}) collective-permute-start(s32[512]{0:T(512)S(1)} %get-tuple-element.772), channel_id=1, source_target_pairs={{0,1},{1,2},{2,3},{3,4},{4,5},{5,6},{6,7},{7,8},{8,9},{9,10},{10,1... | collective-permute-start | bytes 6152 | tf_op jit(solution)/shard_map/while/body/eval_jaxpr/ppermute | solution.py:12
  170.9 14.0 %collective-permute-start.1 = (bf16[512,256]{1,0:T(8,128)(2,1)S(1)}, bf16[512,256]{1,0:T(8,128)(2,1)S(1)}, u32[]{:S(2)}, u32[]{:S(2)}) collective-permute-start(bf16[512,256]{1,0:T(8,128)(2,1)S(1)} %get-tuple-element.771), channel_id=1, source_target_pairs={{0,1},{1,2},{2,3},{3,4},{4,5},{5,6},{6,7},{7,8},{8,9},{9,10},{10,1... | collective-permute-start | bytes 786440 | tf_op jit(solution)/shard_map/while/body/eval_jaxpr/ppermute | solution.py:12
  172.8 8.8 %collective-permute-start = (s32[512]{0:T(512)S(1)}, s32[512]{0:T(512)S(1)}, u32[]{:S(2)}, u32[]{:S(2)}) collective-permute-start(s32[512]{0:T(512)S(1)} %get-tuple-element.772), channel_id=1, source_target_pairs={{0,1},{1,2},{2,3},{3,4},{4,5},{5,6},{6,7},{7,8},{8,9},{9,10},{10,1... | collective-permute-start | bytes 6152 | tf_op jit(solution)/shard_map/while/body/eval_jaxpr/ppermute | solution.py:12
  189.2 14.0 %collective-permute-start.1 = (bf16[512,256]{1,0:T(8,128)(2,1)S(1)}, bf16[512,256]{1,0:T(8,128)(2,1)S(1)}, u32[]{:S(2)}, u32[]{:S(2)}) collective-permute-start(bf16[512,256]{1,0:T(8,128)(2,1)S(1)} %get-tuple-element.771), channel_id=1, source_target_pairs={{0,1},{1,2},{2,3},{3,4},{4,5},{5,6},{6,7},{7,8},{8,9},{9,10},{10,1... | collective-permute-start | bytes 786440 | tf_op jit(solution)/shard_map/while/body/eval_jaxpr/ppermute | solution.py:12
  191.1 8.8 %collective-permute-start = (s32[512]{0:T(512)S(1)}, s32[512]{0:T(512)S(1)}, u32[]{:S(2)}, u32[]{:S(2)}) collective-permute-start(s32[512]{0:T(512)S(1)} %get-tuple-element.772), channel_id=1, source_target_pairs={{0,1},{1,2},{2,3},{3,4},{4,5},{5,6},{6,7},{7,8},{8,9},{9,10},{10,1... | collective-permute-start | bytes 6152 | tf_op jit(solution)/shard_map/while/body/eval_jaxpr/ppermute | solution.py:12
  207.5 18.7 %collective-permute-start.1 = (bf16[512,256]{1,0:T(8,128)(2,1)S(1)}, bf16[512,256]{1,0:T(8,128)(2,1)S(1)}, u32[]{:S(2)}, u32[]{:S(2)}) collective-permute-start(bf16[512,256]{1,0:T(8,128)(2,1)S(1)} %get-tuple-element.771), channel_id=1, source_target_pairs={{0,1},{1,2},{2,3},{3,4},{4,5},{5,6},{6,7},{7,8},{8,9},{9,10},{10,1... | collective-permute-start | bytes 786440 | tf_op jit(solution)/shard_map/while/body/eval_jaxpr/ppermute | solution.py:12
  209.5 13.5 %collective-permute-start = (s32[512]{0:T(512)S(1)}, s32[512]{0:T(512)S(1)}, u32[]{:S(2)}, u32[]{:S(2)}) collective-permute-start(s32[512]{0:T(512)S(1)} %get-tuple-element.772), channel_id=1, source_target_pairs={{0,1},{1,2},{2,3},{3,4},{4,5},{5,6},{6,7},{7,8},{8,9},{9,10},{10,1... | collective-permute-start | bytes 6152 | tf_op jit(solution)/shard_map/while/body/eval_jaxpr/ppermute | solution.py:12
  230.6 12.5 %collective-permute-start.1 = (bf16[512,256]{1,0:T(8,128)(2,1)S(1)}, bf16[512,256]{1,0:T(8,128)(2,1)S(1)}, u32[]{:S(2)}, u32[]{:S(2)}) collective-permute-start(bf16[512,256]{1,0:T(8,128)(2,1)S(1)} %get-tuple-element.771), channel_id=1, source_target_pairs={{0,1},{1,2},{2,3},{3,4},{4,5},{5,6},{6,7},{7,8},{8,9},{9,10},{10,1... | collective-permute-start | bytes 786440 | tf_op jit(solution)/shard_map/while/body/eval_jaxpr/ppermute | solution.py:12
  232.5 7.3 %collective-permute-start = (s32[512]{0:T(512)S(1)}, s32[512]{0:T(512)S(1)}, u32[]{:S(2)}, u32[]{:S(2)}) collective-permute-start(s32[512]{0:T(512)S(1)} %get-tuple-element.772), channel_id=1, source_target_pairs={{0,1},{1,2},{2,3},{3,4},{4,5},{5,6},{6,7},{7,8},{8,9},{9,10},{10,1... | collective-permute-start | bytes 6152 | tf_op jit(solution)/shard_map/while/body/eval_jaxpr/ppermute | solution.py:12
  247.4 13.4 %collective-permute-start.1 = (bf16[512,256]{1,0:T(8,128)(2,1)S(1)}, bf16[512,256]{1,0:T(8,128)(2,1)S(1)}, u32[]{:S(2)}, u32[]{:S(2)}) collective-permute-start(bf16[512,256]{1,0:T(8,128)(2,1)S(1)} %get-tuple-element.771), channel_id=1, source_target_pairs={{0,1},{1,2},{2,3},{3,4},{4,5},{5,6},{6,7},{7,8},{8,9},{9,10},{10,1... | collective-permute-start | bytes 786440 | tf_op jit(solution)/shard_map/while/body/eval_jaxpr/ppermute | solution.py:12
  249.3 8.2 %collective-permute-start = (s32[512]{0:T(512)S(1)}, s32[512]{0:T(512)S(1)}, u32[]{:S(2)}, u32[]{:S(2)}) collective-permute-start(s32[512]{0:T(512)S(1)} %get-tuple-element.772), channel_id=1, source_target_pairs={{0,1},{1,2},{2,3},{3,4},{4,5},{5,6},{6,7},{7,8},{8,9},{9,10},{10,1... | collective-permute-start | bytes 6152 | tf_op jit(solution)/shard_map/while/body/eval_jaxpr/ppermute | solution.py:12
  265.2 17.1 %collective-permute-start.1 = (bf16[512,256]{1,0:T(8,128)(2,1)S(1)}, bf16[512,256]{1,0:T(8,128)(2,1)S(1)}, u32[]{:S(2)}, u32[]{:S(2)}) collective-permute-start(bf16[512,256]{1,0:T(8,128)(2,1)S(1)} %get-tuple-element.771), channel_id=1, source_target_pairs={{0,1},{1,2},{2,3},{3,4},{4,5},{5,6},{6,7},{7,8},{8,9},{9,10},{10,1... | collective-permute-start | bytes 786440 | tf_op jit(solution)/shard_map/while/body/eval_jaxpr/ppermute | solution.py:12
  267.1 11.9 %collective-permute-start = (s32[512]{0:T(512)S(1)}, s32[512]{0:T(512)S(1)}, u32[]{:S(2)}, u32[]{:S(2)}) collective-permute-start(s32[512]{0:T(512)S(1)} %get-tuple-element.772), channel_id=1, source_target_pairs={{0,1},{1,2},{2,3},{3,4},{4,5},{5,6},{6,7},{7,8},{8,9},{9,10},{10,1... | collective-permute-start | bytes 6152 | tf_op jit(solution)/shard_map/while/body/eval_jaxpr/ppermute | solution.py:12
  286.6 13.7 %collective-permute-start.1 = (bf16[512,256]{1,0:T(8,128)(2,1)S(1)}, bf16[512,256]{1,0:T(8,128)(2,1)S(1)}, u32[]{:S(2)}, u32[]{:S(2)}) collective-permute-start(bf16[512,256]{1,0:T(8,128)(2,1)S(1)} %get-tuple-element.771), channel_id=1, source_target_pairs={{0,1},{1,2},{2,3},{3,4},{4,5},{5,6},{6,7},{7,8},{8,9},{9,10},{10,1... | collective-permute-start | bytes 786440 | tf_op jit(solution)/shard_map/while/body/eval_jaxpr/ppermute | solution.py:12
  288.6 8.5 %collective-permute-start = (s32[512]{0:T(512)S(1)}, s32[512]{0:T(512)S(1)}, u32[]{:S(2)}, u32[]{:S(2)}) collective-permute-start(s32[512]{0:T(512)S(1)} %get-tuple-element.772), channel_id=1, source_target_pairs={{0,1},{1,2},{2,3},{3,4},{4,5},{5,6},{6,7},{7,8},{8,9},{9,10},{10,1... | collective-permute-start | bytes 6152 | tf_op jit(solution)/shard_map/while/body/eval_jaxpr/ppermute | solution.py:12
  304.7 14.0 %collective-permute-start.1 = (bf16[512,256]{1,0:T(8,128)(2,1)S(1)}, bf16[512,256]{1,0:T(8,128)(2,1)S(1)}, u32[]{:S(2)}, u32[]{:S(2)}) collective-permute-start(bf16[512,256]{1,0:T(8,128)(2,1)S(1)} %get-tuple-element.771), channel_id=1, source_target_pairs={{0,1},{1,2},{2,3},{3,4},{4,5},{5,6},{6,7},{7,8},{8,9},{9,10},{10,1... | collective-permute-start | bytes 786440 | tf_op jit(solution)/shard_map/while/body/eval_jaxpr/ppermute | solution.py:12
  306.6 8.8 %collective-permute-start = (s32[512]{0:T(512)S(1)}, s32[512]{0:T(512)S(1)}, u32[]{:S(2)}, u32[]{:S(2)}) collective-permute-start(s32[512]{0:T(512)S(1)} %get-tuple-element.772), channel_id=1, source_target_pairs={{0,1},{1,2},{2,3},{3,4},{4,5},{5,6},{6,7},{7,8},{8,9},{9,10},{10,1... | collective-permute-start | bytes 6152 | tf_op jit(solution)/shard_map/while/body/eval_jaxpr/ppermute | solution.py:12
  323.0 15.7 %collective-permute-start.1 = (bf16[512,256]{1,0:T(8,128)(2,1)S(1)}, bf16[512,256]{1,0:T(8,128)(2,1)S(1)}, u32[]{:S(2)}, u32[]{:S(2)}) collective-permute-start(bf16[512,256]{1,0:T(8,128)(2,1)S(1)} %get-tuple-element.771), channel_id=1, source_target_pairs={{0,1},{1,2},{2,3},{3,4},{4,5},{5,6},{6,7},{7,8},{8,9},{9,10},{10,1... | collective-permute-start | bytes 786440 | tf_op jit(solution)/shard_map/while/body/eval_jaxpr/ppermute | solution.py:12
  325.0 10.5 %collective-permute-start = (s32[512]{0:T(512)S(1)}, s32[512]{0:T(512)S(1)}, u32[]{:S(2)}, u32[]{:S(2)}) collective-permute-start(s32[512]{0:T(512)S(1)} %get-tuple-element.772), channel_id=1, source_target_pairs={{0,1},{1,2},{2,3},{3,4},{4,5},{5,6},{6,7},{7,8},{8,9},{9,10},{10,1... | collective-permute-start | bytes 6152 | tf_op jit(solution)/shard_map/while/body/eval_jaxpr/ppermute | solution.py:12
  343.1 13.7 %collective-permute-start.1 = (bf16[512,256]{1,0:T(8,128)(2,1)S(1)}, bf16[512,256]{1,0:T(8,128)(2,1)S(1)}, u32[]{:S(2)}, u32[]{:S(2)}) collective-permute-start(bf16[512,256]{1,0:T(8,128)(2,1)S(1)} %get-tuple-element.771), channel_id=1, source_target_pairs={{0,1},{1,2},{2,3},{3,4},{4,5},{5,6},{6,7},{7,8},{8,9},{9,10},{10,1... | collective-permute-start | bytes 786440 | tf_op jit(solution)/shard_map/while/body/eval_jaxpr/ppermute | solution.py:12
  345.0 8.5 %collective-permute-start = (s32[512]{0:T(512)S(1)}, s32[512]{0:T(512)S(1)}, u32[]{:S(2)}, u32[]{:S(2)}) collective-permute-start(s32[512]{0:T(512)S(1)} %get-tuple-element.772), channel_id=1, source_target_pairs={{0,1},{1,2},{2,3},{3,4},{4,5},{5,6},{6,7},{7,8},{8,9},{9,10},{10,1... | collective-permute-start | bytes 6152 | tf_op jit(solution)/shard_map/while/body/eval_jaxpr/ppermute | solution.py:12
  361.1 12.6 %collective-permute-start.1 = (bf16[512,256]{1,0:T(8,128)(2,1)S(1)}, bf16[512,256]{1,0:T(8,128)(2,1)S(1)}, u32[]{:S(2)}, u32[]{:S(2)}) collective-permute-start(bf16[512,256]{1,0:T(8,128)(2,1)S(1)} %get-tuple-element.771), channel_id=1, source_target_pairs={{0,1},{1,2},{2,3},{3,4},{4,5},{5,6},{6,7},{7,8},{8,9},{9,10},{10,1... | collective-permute-start | bytes 786440 | tf_op jit(solution)/shard_map/while/body/eval_jaxpr/ppermute | solution.py:12
  363.0 7.4 %collective-permute-start = (s32[512]{0:T(512)S(1)}, s32[512]{0:T(512)S(1)}, u32[]{:S(2)}, u32[]{:S(2)}) collective-permute-start(s32[512]{0:T(512)S(1)} %get-tuple-element.772), channel_id=1, source_target_pairs={{0,1},{1,2},{2,3},{3,4},{4,5},{5,6},{6,7},{7,8},{8,9},{9,10},{10,1... | collective-permute-start | bytes 6152 | tf_op jit(solution)/shard_map/while/body/eval_jaxpr/ppermute | solution.py:12
  378.0 16.7 %collective-permute-start.1 = (bf16[512,256]{1,0:T(8,128)(2,1)S(1)}, bf16[512,256]{1,0:T(8,128)(2,1)S(1)}, u32[]{:S(2)}, u32[]{:S(2)}) collective-permute-start(bf16[512,256]{1,0:T(8,128)(2,1)S(1)} %get-tuple-element.771), channel_id=1, source_target_pairs={{0,1},{1,2},{2,3},{3,4},{4,5},{5,6},{6,7},{7,8},{8,9},{9,10},{10,1... | collective-permute-start | bytes 786440 | tf_op jit(solution)/shard_map/while/body/eval_jaxpr/ppermute | solution.py:12
  380.0 11.5 %collective-permute-start = (s32[512]{0:T(512)S(1)}, s32[512]{0:T(512)S(1)}, u32[]{:S(2)}, u32[]{:S(2)}) collective-permute-start(s32[512]{0:T(512)S(1)} %get-tuple-element.772), channel_id=1, source_target_pairs={{0,1},{1,2},{2,3},{3,4},{4,5},{5,6},{6,7},{7,8},{8,9},{9,10},{10,1... | collective-permute-start | bytes 6152 | tf_op jit(solution)/shard_map/while/body/eval_jaxpr/ppermute | solution.py:12
  399.1 14.8 %collective-permute-start.1 = (bf16[512,256]{1,0:T(8,128)(2,1)S(1)}, bf16[512,256]{1,0:T(8,128)(2,1)S(1)}, u32[]{:S(2)}, u32[]{:S(2)}) collective-permute-start(bf16[512,256]{1,0:T(8,128)(2,1)S(1)} %get-tuple-element.771), channel_id=1, source_target_pairs={{0,1},{1,2},{2,3},{3,4},{4,5},{5,6},{6,7},{7,8},{8,9},{9,10},{10,1... | collective-permute-start | bytes 786440 | tf_op jit(solution)/shard_map/while/body/eval_jaxpr/ppermute | solution.py:12
  401.0 9.6 %collective-permute-start = (s32[512]{0:T(512)S(1)}, s32[512]{0:T(512)S(1)}, u32[]{:S(2)}, u32[]{:S(2)}) collective-permute-start(s32[512]{0:T(512)S(1)} %get-tuple-element.772), channel_id=1, source_target_pairs={{0,1},{1,2},{2,3},{3,4},{4,5},{5,6},{6,7},{7,8},{8,9},{9,10},{10,1... | collective-permute-start | bytes 6152 | tf_op jit(solution)/shard_map/while/body/eval_jaxpr/ppermute | solution.py:12
  418.2 15.0 %collective-permute-start.1 = (bf16[512,256]{1,0:T(8,128)(2,1)S(1)}, bf16[512,256]{1,0:T(8,128)(2,1)S(1)}, u32[]{:S(2)}, u32[]{:S(2)}) collective-permute-start(bf16[512,256]{1,0:T(8,128)(2,1)S(1)} %get-tuple-element.771), channel_id=1, source_target_pairs={{0,1},{1,2},{2,3},{3,4},{4,5},{5,6},{6,7},{7,8},{8,9},{9,10},{10,1... | collective-permute-start | bytes 786440 | tf_op jit(solution)/shard_map/while/body/eval_jaxpr/ppermute | solution.py:12
  420.2 9.8 %collective-permute-start = (s32[512]{0:T(512)S(1)}, s32[512]{0:T(512)S(1)}, u32[]{:S(2)}, u32[]{:S(2)}) collective-permute-start(s32[512]{0:T(512)S(1)} %get-tuple-element.772), channel_id=1, source_target_pairs={{0,1},{1,2},{2,3},{3,4},{4,5},{5,6},{6,7},{7,8},{8,9},{9,10},{10,1... | collective-permute-start | bytes 6152 | tf_op jit(solution)/shard_map/while/body/eval_jaxpr/ppermute | solution.py:12
  437.6 14.0 %collective-permute-start.1 = (bf16[512,256]{1,0:T(8,128)(2,1)S(1)}, bf16[512,256]{1,0:T(8,128)(2,1)S(1)}, u32[]{:S(2)}, u32[]{:S(2)}) collective-permute-start(bf16[512,256]{1,0:T(8,128)(2,1)S(1)} %get-tuple-element.771), channel_id=1, source_target_pairs={{0,1},{1,2},{2,3},{3,4},{4,5},{5,6},{6,7},{7,8},{8,9},{9,10},{10,1... | collective-permute-start | bytes 786440 | tf_op jit(solution)/shard_map/while/body/eval_jaxpr/ppermute | solution.py:12
  439.5 8.8 %collective-permute-start = (s32[512]{0:T(512)S(1)}, s32[512]{0:T(512)S(1)}, u32[]{:S(2)}, u32[]{:S(2)}) collective-permute-start(s32[512]{0:T(512)S(1)} %get-tuple-element.772), channel_id=1, source_target_pairs={{0,1},{1,2},{2,3},{3,4},{4,5},{5,6},{6,7},{7,8},{8,9},{9,10},{10,1... | collective-permute-start | bytes 6152 | tf_op jit(solution)/shard_map/while/body/eval_jaxpr/ppermute | solution.py:12
  455.9 14.9 %collective-permute-start.1 = (bf16[512,256]{1,0:T(8,128)(2,1)S(1)}, bf16[512,256]{1,0:T(8,128)(2,1)S(1)}, u32[]{:S(2)}, u32[]{:S(2)}) collective-permute-start(bf16[512,256]{1,0:T(8,128)(2,1)S(1)} %get-tuple-element.771), channel_id=1, source_target_pairs={{0,1},{1,2},{2,3},{3,4},{4,5},{5,6},{6,7},{7,8},{8,9},{9,10},{10,1... | collective-permute-start | bytes 786440 | tf_op jit(solution)/shard_map/while/body/eval_jaxpr/ppermute | solution.py:12
  457.9 9.7 %collective-permute-start = (s32[512]{0:T(512)S(1)}, s32[512]{0:T(512)S(1)}, u32[]{:S(2)}, u32[]{:S(2)}) collective-permute-start(s32[512]{0:T(512)S(1)} %get-tuple-element.772), channel_id=1, source_target_pairs={{0,1},{1,2},{2,3},{3,4},{4,5},{5,6},{6,7},{7,8},{8,9},{9,10},{10,1... | collective-permute-start | bytes 6152 | tf_op jit(solution)/shard_map/while/body/eval_jaxpr/ppermute | solution.py:12
  475.2 12.4 %collective-permute-start.1 = (bf16[512,256]{1,0:T(8,128)(2,1)S(1)}, bf16[512,256]{1,0:T(8,128)(2,1)S(1)}, u32[]{:S(2)}, u32[]{:S(2)}) collective-permute-start(bf16[512,256]{1,0:T(8,128)(2,1)S(1)} %get-tuple-element.771), channel_id=1, source_target_pairs={{0,1},{1,2},{2,3},{3,4},{4,5},{5,6},{6,7},{7,8},{8,9},{9,10},{10,1... | collective-permute-start | bytes 786440 | tf_op jit(solution)/shard_map/while/body/eval_jaxpr/ppermute | solution.py:12
  477.1 7.3 %collective-permute-start = (s32[512]{0:T(512)S(1)}, s32[512]{0:T(512)S(1)}, u32[]{:S(2)}, u32[]{:S(2)}) collective-permute-start(s32[512]{0:T(512)S(1)} %get-tuple-element.772), channel_id=1, source_target_pairs={{0,1},{1,2},{2,3},{3,4},{4,5},{5,6},{6,7},{7,8},{8,9},{9,10},{10,1... | collective-permute-start | bytes 6152 | tf_op jit(solution)/shard_map/while/body/eval_jaxpr/ppermute | solution.py:12
  492.0 12.5 %collective-permute-start.1 = (bf16[512,256]{1,0:T(8,128)(2,1)S(1)}, bf16[512,256]{1,0:T(8,128)(2,1)S(1)}, u32[]{:S(2)}, u32[]{:S(2)}) collective-permute-start(bf16[512,256]{1,0:T(8,128)(2,1)S(1)} %get-tuple-element.771), channel_id=1, source_target_pairs={{0,1},{1,2},{2,3},{3,4},{4,5},{5,6},{6,7},{7,8},{8,9},{9,10},{10,1... | collective-permute-start | bytes 786440 | tf_op jit(solution)/shard_map/while/body/eval_jaxpr/ppermute | solution.py:12
  493.9 7.3 %collective-permute-start = (s32[512]{0:T(512)S(1)}, s32[512]{0:T(512)S(1)}, u32[]{:S(2)}, u32[]{:S(2)}) collective-permute-start(s32[512]{0:T(512)S(1)} %get-tuple-element.772), channel_id=1, source_target_pairs={{0,1},{1,2},{2,3},{3,4},{4,5},{5,6},{6,7},{7,8},{8,9},{9,10},{10,1... | collective-permute-start | bytes 6152 | tf_op jit(solution)/shard_map/while/body/eval_jaxpr/ppermute | solution.py:12
  508.9 12.4 %collective-permute-start.1 = (bf16[512,256]{1,0:T(8,128)(2,1)S(1)}, bf16[512,256]{1,0:T(8,128)(2,1)S(1)}, u32[]{:S(2)}, u32[]{:S(2)}) collective-permute-start(bf16[512,256]{1,0:T(8,128)(2,1)S(1)} %get-tuple-element.771), channel_id=1, source_target_pairs={{0,1},{1,2},{2,3},{3,4},{4,5},{5,6},{6,7},{7,8},{8,9},{9,10},{10,1... | collective-permute-start | bytes 786440 | tf_op jit(solution)/shard_map/while/body/eval_jaxpr/ppermute | solution.py:12
  510.8 7.3 %collective-permute-start = (s32[512]{0:T(512)S(1)}, s32[512]{0:T(512)S(1)}, u32[]{:S(2)}, u32[]{:S(2)}) collective-permute-start(s32[512]{0:T(512)S(1)} %get-tuple-element.772), channel_id=1, source_target_pairs={{0,1},{1,2},{2,3},{3,4},{4,5},{5,6},{6,7},{7,8},{8,9},{9,10},{10,1... | collective-permute-start | bytes 6152 | tf_op jit(solution)/shard_map/while/body/eval_jaxpr/ppermute | solution.py:12
  525.7 13.8 %collective-permute-start.1 = (bf16[512,256]{1,0:T(8,128)(2,1)S(1)}, bf16[512,256]{1,0:T(8,128)(2,1)S(1)}, u32[]{:S(2)}, u32[]{:S(2)}) collective-permute-start(bf16[512,256]{1,0:T(8,128)(2,1)S(1)} %get-tuple-element.771), channel_id=1, source_target_pairs={{0,1},{1,2},{2,3},{3,4},{4,5},{5,6},{6,7},{7,8},{8,9},{9,10},{10,1... | collective-permute-start | bytes 786440 | tf_op jit(solution)/shard_map/while/body/eval_jaxpr/ppermute | solution.py:12
  527.6 8.7 %collective-permute-start = (s32[512]{0:T(512)S(1)}, s32[512]{0:T(512)S(1)}, u32[]{:S(2)}, u32[]{:S(2)}) collective-permute-start(s32[512]{0:T(512)S(1)} %get-tuple-element.772), channel_id=1, source_target_pairs={{0,1},{1,2},{2,3},{3,4},{4,5},{5,6},{6,7},{7,8},{8,9},{9,10},{10,1... | collective-permute-start | bytes 6152 | tf_op jit(solution)/shard_map/while/body/eval_jaxpr/ppermute | solution.py:12
  543.9 14.4 %collective-permute-start.1 = (bf16[512,256]{1,0:T(8,128)(2,1)S(1)}, bf16[512,256]{1,0:T(8,128)(2,1)S(1)}, u32[]{:S(2)}, u32[]{:S(2)}) collective-permute-start(bf16[512,256]{1,0:T(8,128)(2,1)S(1)} %get-tuple-element.771), channel_id=1, source_target_pairs={{0,1},{1,2},{2,3},{3,4},{4,5},{5,6},{6,7},{7,8},{8,9},{9,10},{10,1... | collective-permute-start | bytes 786440 | tf_op jit(solution)/shard_map/while/body/eval_jaxpr/ppermute | solution.py:12
  545.8 9.2 %collective-permute-start = (s32[512]{0:T(512)S(1)}, s32[512]{0:T(512)S(1)}, u32[]{:S(2)}, u32[]{:S(2)}) collective-permute-start(s32[512]{0:T(512)S(1)} %get-tuple-element.772), channel_id=1, source_target_pairs={{0,1},{1,2},{2,3},{3,4},{4,5},{5,6},{6,7},{7,8},{8,9},{9,10},{10,1... | collective-permute-start | bytes 6152 | tf_op jit(solution)/shard_map/while/body/eval_jaxpr/ppermute | solution.py:12
  562.6 16.1 %collective-permute-start.1 = (bf16[512,256]{1,0:T(8,128)(2,1)S(1)}, bf16[512,256]{1,0:T(8,128)(2,1)S(1)}, u32[]{:S(2)}, u32[]{:S(2)}) collective-permute-start(bf16[512,256]{1,0:T(8,128)(2,1)S(1)} %get-tuple-element.771), channel_id=1, source_target_pairs={{0,1},{1,2},{2,3},{3,4},{4,5},{5,6},{6,7},{7,8},{8,9},{9,10},{10,1... | collective-permute-start | bytes 786440 | tf_op jit(solution)/shard_map/while/body/eval_jaxpr/ppermute | solution.py:12
  564.5 10.9 %collective-permute-start = (s32[512]{0:T(512)S(1)}, s32[512]{0:T(512)S(1)}, u32[]{:S(2)}, u32[]{:S(2)}) collective-permute-start(s32[512]{0:T(512)S(1)} %get-tuple-element.772), channel_id=1, source_target_pairs={{0,1},{1,2},{2,3},{3,4},{4,5},{5,6},{6,7},{7,8},{8,9},{9,10},{10,1... | collective-permute-start | bytes 6152 | tf_op jit(solution)/shard_map/while/body/eval_jaxpr/ppermute | solution.py:12
  583.0 12.4 %collective-permute-start.1 = (bf16[512,256]{1,0:T(8,128)(2,1)S(1)}, bf16[512,256]{1,0:T(8,128)(2,1)S(1)}, u32[]{:S(2)}, u32[]{:S(2)}) collective-permute-start(bf16[512,256]{1,0:T(8,128)(2,1)S(1)} %get-tuple-element.771), channel_id=1, source_target_pairs={{0,1},{1,2},{2,3},{3,4},{4,5},{5,6},{6,7},{7,8},{8,9},{9,10},{10,1... | collective-permute-start | bytes 786440 | tf_op jit(solution)/shard_map/while/body/eval_jaxpr/ppermute | solution.py:12
  599.8 13.9 %collective-permute-start.1 = (bf16[512,256]{1,0:T(8,128)(2,1)S(1)}, bf16[512,256]{1,0:T(8,128)(2,1)S(1)}, u32[]{:S(2)}, u32[]{:S(2)}) collective-permute-start(bf16[512,256]{1,0:T(8,128)(2,1)S(1)} %get-tuple-element.771), channel_id=1, source_target_pairs={{0,1},{1,2},{2,3},{3,4},{4,5},{5,6},{6,7},{7,8},{8,9},{9,10},{10,1... | collective-permute-start | bytes 786440 | tf_op jit(solution)/shard_map/while/body/eval_jaxpr/ppermute | solution.py:12
  601.8 8.7 %collective-permute-start = (s32[512]{0:T(512)S(1)}, s32[512]{0:T(512)S(1)}, u32[]{:S(2)}, u32[]{:S(2)}) collective-permute-start(s32[512]{0:T(512)S(1)} %get-tuple-element.772), channel_id=1, source_target_pairs={{0,1},{1,2},{2,3},{3,4},{4,5},{5,6},{6,7},{7,8},{8,9},{9,10},{10,1... | collective-permute-start | bytes 6152 | tf_op jit(solution)/shard_map/while/body/eval_jaxpr/ppermute | solution.py:12
  618.1 14.0 %collective-permute-start.1 = (bf16[512,256]{1,0:T(8,128)(2,1)S(1)}, bf16[512,256]{1,0:T(8,128)(2,1)S(1)}, u32[]{:S(2)}, u32[]{:S(2)}) collective-permute-start(bf16[512,256]{1,0:T(8,128)(2,1)S(1)} %get-tuple-element.771), channel_id=1, source_target_pairs={{0,1},{1,2},{2,3},{3,4},{4,5},{5,6},{6,7},{7,8},{8,9},{9,10},{10,1... | collective-permute-start | bytes 786440 | tf_op jit(solution)/shard_map/while/body/eval_jaxpr/ppermute | solution.py:12
  620.0 8.8 %collective-permute-start = (s32[512]{0:T(512)S(1)}, s32[512]{0:T(512)S(1)}, u32[]{:S(2)}, u32[]{:S(2)}) collective-permute-start(s32[512]{0:T(512)S(1)} %get-tuple-element.772), channel_id=1, source_target_pairs={{0,1},{1,2},{2,3},{3,4},{4,5},{5,6},{6,7},{7,8},{8,9},{9,10},{10,1... | collective-permute-start | bytes 6152 | tf_op jit(solution)/shard_map/while/body/eval_jaxpr/ppermute | solution.py:12
  (5 other events, 75.5 us)
where the time goes:
time: 642 us; the launch traced here: 638 us
  waiting for transfers between devices  171 us (27%)
  starting transfers between devices  141 us (22%)
  loops' own time  128 us (20%)
  matrix products  96.6 us (15%)
  other arithmetic  51.2 us (8%)
  local copies, waits for them, and re-layouts  45.6 us (7%)
    ppermute x64, waiting for transfers between devices, shifted(): lax.ppermute(value, axis, [(source, source + steps) for source in range(l...  158 us
    ppermute x64, starting transfers between devices, shifted(): lax.ppermute(value, axis, [(source, source + steps) for source in range(l...  130 us
    another operation x1, loops' own time, local(): lax.fori_loop(0, device_reach, travel, (own_state, kv_seq, segment_ids))[0]  126 us
    dot_general x33, matrix products, update(): jnp.einsum('hqk,kd->qhd', weights.astype(jnp.bfloat16), value_part, prefe...  63.1 us
    reduce_sum x33, other arithmetic, update(): denominator = denominator * factor + jnp.sum(weights, axis=-1)  34.3 us
    dot_general x33, matrix products, update(): jnp.einsum('qhd,kd->hqk', queries, key_part, preferred_element_type=jnp.f...  29 us
    slice x32, local copies, waits for them, and re-layouts, one_block(): seg_now[0] <= last_seg  21.2 us
    slice x32, local copies, waits for them, and re-layouts, one_block(): pos_now[0] <= last_pos  16.4 us
  transfers between devices with their start and end apart: 66, of which 34 were waited for; matrix products, arithmetic and copies ran while one was open for 7% of the time, Pallas kernels for 0%

commit v1 on v0

v1 whole, which is shorter than its diff:
```python
import math

import jax
import jax.numpy as jnp
from jax import lax
from jax.experimental import pallas as pl
from jax.experimental.pallas import tpu as pltpu
from jax.sharding import PartitionSpec as P


def shifted(value, axis, steps):
    count = lax.axis_size(axis)
    leading, last = (max(0, -steps), min(count, count - steps))
    return lax.ppermute(value, axis, [(source, source + steps) for source in range(leading, last)])


def select_rows(selector, blocks, pattern):
    return jnp.einsum(
        pattern, selector.astype(jnp.bfloat16), blocks, preferred_element_type=jnp.float32
    ).astype(jnp.bfloat16)


def local(q_load, kv_load, pack_dest, counts, segment_ids):
    group_width = lax.axis_size("inner")
    my_index = lax.axis_index("inner")
    capacity = pack_dest.shape[1]
    slot_count = capacity // 2
    pair_limit = -(-capacity // group_width)
    row_length = q_load.shape[0] // capacity
    query_width = q_load.shape[1]
    pair_width = kv_load.shape[1]
    head_size = pair_width // 2
    head_count = query_width // head_size
    slot_grid = lax.broadcasted_iota(jnp.int32, (group_width, capacity), 1)
    live_all = slot_grid < counts[:, None]
    owner_all = pack_dest // slot_count
    slot_numbers = jnp.arange(capacity, dtype=jnp.int32)
    earlier = slot_numbers[None, :] < slot_numbers[:, None]
    same_owner = owner_all[:, :, None] == owner_all[:, None, :]
    rank_all = jnp.sum(
        (earlier[None] & same_owner & live_all[:, None, :]).astype(jnp.int32), axis=2
    )
    shard_rows = jnp.arange(group_width, dtype=jnp.int32)
    mine_row = (shard_rows == my_index)[:, None]
    my_owner = jnp.sum(jnp.where(mine_row, owner_all, 0), axis=0)
    my_rank = jnp.sum(jnp.where(mine_row, rank_all, 0), axis=0)
    my_live = jnp.any(mine_row & live_all, axis=0)
    pair_ids = jnp.arange(pair_limit, dtype=jnp.int32)
    send_select = (
        my_live[None, None, :]
        & (my_owner[None, None, :] == shard_rows[:, None, None])
        & (my_rank[None, None, :] == pair_ids[None, :, None])
    )
    q_blocks = q_load.reshape(capacity, row_length, query_width)
    kv_blocks = kv_load.reshape(capacity, row_length, pair_width)
    send_q = select_rows(send_select, q_blocks, "jkc,crf->jkrf")
    send_kv = select_rows(send_select, kv_blocks, "jkc,crf->jkrf")
    recv_q, recv_kv = (
        lax.all_to_all(send_q, "inner", split_axis=0, concat_axis=0, tiled=True),
        lax.all_to_all(send_kv, "inner", split_axis=0, concat_axis=0, tiled=True),
    )
    wanted = my_index * slot_count + jnp.arange(slot_count, dtype=jnp.int32)
    take_select = jnp.any(
        live_all[None, :, None, :]
        & (pack_dest[None, :, None, :] == wanted[:, None, None, None])
        & (rank_all[None, :, None, :] == pair_ids[None, None, :, None]),
        axis=3,
    )
    q_seq = select_rows(take_select, recv_q, "srk,rktf->stf").reshape(
        slot_count * row_length, query_width
    )
    kv_seq = select_rows(take_select, recv_kv, "srk,rktf->stf").reshape(
        slot_count * row_length, pair_width
    )
    tok_rows = q_seq.shape[0]
    owner_index = lax.axis_index(("outer", "inner"))
    outer_index = lax.axis_index("outer")
    score_scale = 1.0 / math.sqrt(head_size)
    extra_rows = 16
    seg_rows = tok_rows // pair_width
    seg_pad = jnp.zeros((extra_rows - seg_rows, pair_width), jnp.bfloat16)
    packed = jnp.concatenate(
        [kv_seq, segment_ids.astype(jnp.bfloat16).reshape(seg_rows, pair_width), seg_pad], axis=0
    )
    outer_reach = -(-(lax.axis_size("outer") * group_width // 4) // group_width)
    moved = [packed] + [shifted(packed, "outer", step) for step in range(1, outer_reach + 1)]
    chunks = lax.all_gather(jnp.stack(moved), "inner", tiled=False)
    chunk_count = outer_reach + 1
    block_count = chunk_count * group_width
    block_ids = jnp.arange(block_count, dtype=jnp.int32)
    key_device = (outer_index - block_ids // group_width) * group_width + block_ids % group_width
    flat_seg = chunks[:, :, tok_rows : tok_rows + seg_rows, :]
    key_first = jnp.transpose(flat_seg[:, :, 0, 0]).reshape(block_count)
    key_last = jnp.transpose(flat_seg[:, :, seg_rows - 1, pair_width - 1]).reshape(block_count)
    first_seg = segment_ids[0].astype(jnp.bfloat16)
    last_seg = segment_ids[tok_rows - 1].astype(jnp.bfloat16)
    needed = (
        (key_device >= 0)
        & (key_device <= owner_index)
        & (key_last >= first_seg)
        & (key_first <= last_seg)
    ).astype(jnp.int32)
    meta = jnp.concatenate([owner_index.reshape(1).astype(jnp.int32), needed])
    query_seg = segment_ids.astype(jnp.float32).reshape(tok_rows, 1)
    return attend(meta, q_seq, query_seg, chunks, head_count, head_size, score_scale)


def attend(meta, q_seq, query_seg, chunks, head_count, head_size, score_scale):
    tok_rows = q_seq.shape[0]
    group_width, chunk_count, packed_rows, pair_width = chunks.shape
    block_count = group_width * chunk_count
    seg_rows = tok_rows // pair_width

    def kernel(meta_ref, q_ref, qseg_ref, kv_ref, out_ref, m_ref, l_ref, acc_ref):
        b = pl.program_id(0)

        @pl.when(b == 0)
        def _():
            m_ref[...] = jnp.full(m_ref.shape, -1e30, jnp.float32)
            l_ref[...] = jnp.zeros(l_ref.shape, jnp.float32)
            acc_ref[...] = jnp.zeros(acc_ref.shape, jnp.float32)

        @pl.when(meta_ref[1 + b] == 1)
        def _():
            own = meta_ref[0]
            chunk = b // group_width
            device = (own // group_width - chunk) * group_width + b % group_width
            seg_parts = [
                kv_ref[0, 0, tok_rows + r : tok_rows + r + 1, :].astype(jnp.float32)
                for r in range(seg_rows)
            ]
            key_seg = jnp.concatenate(seg_parts, axis=1)
            key_pos = device * tok_rows + lax.broadcasted_iota(jnp.int32, (1, tok_rows), 1)
            query_pos = own * tok_rows + lax.broadcasted_iota(jnp.int32, (tok_rows, 1), 0)
            visible = (key_pos <= query_pos) & (key_seg == qseg_ref[...])
            keys = kv_ref[0, 0, :tok_rows, :head_size]
            values = kv_ref[0, 0, :tok_rows, head_size:]
            for h in range(head_count):
                queries = q_ref[:, h * head_size : (h + 1) * head_size]
                scores = lax.dot_general(
                    queries, keys, (((1,), (1,)), ((), ())), preferred_element_type=jnp.float32
                ) * score_scale
                masked = jnp.where(visible, scores, -1e30)
                m_prev = m_ref[h]
                m_next = jnp.maximum(m_prev, jnp.max(masked, axis=1, keepdims=True))
                factor = jnp.exp(m_prev - m_next)
                weights = jnp.where(visible, jnp.exp(masked - m_next[:, :1]), 0.0)
                l_ref[h] = l_ref[h] * factor + jnp.sum(weights, axis=1, keepdims=True)
                acc_ref[h] = acc_ref[h] * factor + jnp.dot(
                    weights.astype(jnp.bfloat16), values, preferred_element_type=jnp.float32
                )
                m_ref[h] = m_next

        @pl.when(b == block_count - 1)
        def _():
            for h in range(head_count):
                out_ref[:, h * head_size : (h + 1) * head_size] = (
                    acc_ref[h] / l_ref[h]
                ).astype(out_ref.dtype)

    grid_spec = pltpu.PrefetchScalarGridSpec(
        num_scalar_prefetch=1,
        grid=(block_count,),
        in_specs=[
            pl.BlockSpec(q_seq.shape, lambda b, meta: (0, 0)),
            pl.BlockSpec(query_seg.shape, lambda b, meta: (0, 0)),
            pl.BlockSpec(
                (1, 1, packed_rows, pair_width),
                lambda b, meta: (b % group_width, b // group_width, 0, 0),
            ),
        ],
        out_specs=pl.BlockSpec(q_seq.shape, lambda b, meta: (0, 0)),
        scratch_shapes=[
            pltpu.VMEM((head_count, tok_rows, head_size), jnp.float32),
            pltpu.VMEM((head_count, tok_rows, head_size), jnp.float32),
            pltpu.VMEM((head_count, tok_rows, head_size), jnp.float32),
        ],
    )
    flops = 4 * block_count * tok_rows * tok_rows * head_size * head_count
    return pl.pallas_call(
        kernel,
        grid_spec=grid_spec,
        out_shape=jax.ShapeDtypeStruct(q_seq.shape, q_seq.dtype),
        compiler_params=pltpu.CompilerParams(dimension_semantics=("arbitrary",)),
        cost_estimate=pl.CostEstimate(
            flops=flops,
            transcendentals=block_count * tok_rows * tok_rows * head_count,
            bytes_accessed=chunks.size * 2 + q_seq.size * 4,
        ),
    )(meta, q_seq, query_seg, chunks)


def solution(mesh):
    in_specs = (
        P(("outer", "inner"), None),
        P(("outer", "inner"), None),
        P("outer", None),
        P("outer"),
        P(("outer", "inner")),
    )
    out_specs = P(("outer", "inner"), None)
    return jax.shard_map(local, mesh=mesh, in_specs=in_specs, out_specs=out_specs, check_vma=False)
```

time: 642 us -> 400 us (0.62)
  the two profiles are of different devices: /device:TPU:74 before, /device:TPU:107 now
where the time goes in v1:
time: 400 us; the launch traced here: 397 us
  waiting for transfers between devices  234 us (58%)
  Pallas kernels  110 us (28%)
  starting transfers between devices  21.8 us (5%)
  between operations  13.6 us (3%)
  other arithmetic  7.61 us (2%)
  local copies, waits for them, and re-layouts  6.24 us (2%)
    all_gather x1, waiting for transfers between devices, local(): chunks = lax.all_gather(jnp.stack(moved), 'inner', tiled=False)  187 us
    pallas_call x1, Pallas kernels, attend(): pl.pallas_call(kernel, grid_spec=grid_spec, out_shape=jax.ShapeDtypeStruc...  110 us
    all_to_all x1, waiting for transfers between devices, local(): lax.all_to_all(send_q, 'inner', split_axis=0, concat_axis=0, tiled=True)  28.4 us
    ppermute x4, starting transfers between devices, shifted(): lax.ppermute(value, axis, [(source, source + steps) for source in range(l...  12 us
    ppermute x4, waiting for transfers between devices, shifted(): lax.ppermute(value, axis, [(source, source + steps) for source in range(l...  11.9 us
  transfers between devices with their start and end apart: 7, of which 6 were waited for; matrix products, arithmetic and copies ran while one was open for 1% of the time, Pallas kernels for 0%

profile of v1, /device:TPU:107, one launch (start us, length us, event | category | flops | bytes accessed | tf_op | source)
XLA Modules:
  0.0 397.2 jit_solution(12337904519578717048)
XLA Ops:
  6.5 0.0 copy-start
  6.5 0.8 add_select_fusion
  7.3 0.7 and_reduce_fusion.1
  8.1 0.3 convert_reduce_fusion
  8.4 0.8 select_reduce_fusion
  9.1 0.0 copy-start.3
  9.1 0.0 copy-start.2
  9.2 1.4 fusion.1
  10.6 0.9 copy.30
  11.5 5.2 %all-to-all-start = ((bf16[8,1,128,256]{3,2,1,0:T(8,128)(2,1)}), bf16[8,1,128,256]{3,2,1,0:T(8,128)(2,1)S(1)}, u32[]{:S(2)}, u32[]{:S(2)}) async-start(bf16[8,1,128,256]{3,2,1,0:T(8,128)(2,1)} %copy.30), calls=%async_computation | async-start | bytes 1048576 | tf_op jit(solution)/shard_map/all_to_all | solution.py:60
  16.7 0.0 all-gather.3.cloned.1.call-start
  16.7 0.0 copy-done.3
  16.7 0.1 pad.4.clone
  16.8 0.0 copy-done.2
  16.8 0.2 and_reduce_fusion
  17.0 6.7 %all-to-all-done = bf16[8,1,128,256]{3,2,1,0:T(8,128)(2,1)S(1)} async-done(((bf16[8,1,128,256]{3,2,1,0:T(8,128)(2,1)}), bf16[8,1,128,256]{3,2,1,0:T(8,128)(2,1)S(1)}, u32[]{:S(2)}, u32[]{:S(2)}) %all-to-all-start) | async-done | bytes 524320 | tf_op jit(solution)/shard_map/all_to_all | solution.py:60
  23.8 0.4 convolution_convert_fusion.3
  24.2 0.1 maximum_maximum_fusion
  24.4 5.3 %collective-permute-start = (bf16[528,256]{1,0:T(8,128)(2,1)S(1)}, bf16[528,256]{1,0:T(8,128)(2,1)S(1)}, u32[]{:S(2)}, u32[]{:S(2)}) collective-permute-start(bf16[528,256]{1,0:T(8,128)(2,1)S(1)} %maximum_maximum_fusion), channel_id=1, source_target_pairs={{0,8},{8,16},{16,24},{24,32},{32,40},{40,48},{48,56},{56,64},{64,7... | collective-permute-start | bytes 811016 | tf_op jit(solution)/shard_map/ppermute | solution.py:14
  29.6 2.9 collective-permute-start.1
  32.5 0.1 bitcast_dynamic-update-slice_fusion.4
  32.7 1.9 collective-permute-start.2
  34.6 1.9 collective-permute-start.3
  36.5 0.0 collective-permute-done
  36.6 3.1 collective-permute-done.1
  39.7 5.4 %collective-permute-done.2 = bf16[528,256]{1,0:T(8,128)(2,1)S(1)} collective-permute-done((bf16[528,256]{1,0:T(8,128)(2,1)S(1)}, bf16[528,256]{1,0:T(8,128)(2,1)S(1)}, u32[]{:S(2)}, u32[]{:S(2)}) %collective-permute-start.2) | collective-permute-done | bytes 270368 | tf_op jit(solution)/shard_map/ppermute | solution.py:14
  45.2 3.3 collective-permute-done.3
  48.5 0.0 copy-start.1
  48.5 1.1 copy-done.1
  49.6 0.0 all-gather.3.cloned.1.call-update
  49.6 0.0 copy-done
  49.6 0.7 fusion
  50.3 1.3 copy.36
  51.7 4.7 %all-to-all-start.1 = ((bf16[8,1,128,512]{3,2,1,0:T(8,128)(2,1)}), bf16[8,1,128,512]{3,2,1,0:T(8,128)(2,1)S(1)}, u32[]{:S(2)}, u32[]{:S(2)}) async-start(bf16[8,1,128,512]{3,2,1,0:T(8,128)(2,1)} %copy.36), calls=%async_computation.1 | async-start | bytes 2097152 | tf_op jit(solution)/shard_map/all_to_all | solution.py:59
  56.3 0.9 copy.39.qseg_ref
  57.2 0.6 fusion.27
  57.8 28.4 %all-to-all-done.1 = bf16[8,1,128,512]{3,2,1,0:T(8,128)(2,1)S(1)} async-done(((bf16[8,1,128,512]{3,2,1,0:T(8,128)(2,1)}), bf16[8,1,128,512]{3,2,1,0:T(8,128)(2,1)S(1)}, u32[]{:S(2)}, u32[]{:S(2)}) %all-to-all-start.1) | async-done | bytes 1048608 | tf_op jit(solution)/shard_map/all_to_all | solution.py:59
  86.1 0.7 convolution_convert_fusion.1
  86.9 0.9 copy.38
  87.8 187.4 %all-gather.3.cloned.1.call-done = bf16[40,528,256]{2,1,0:T(8,128)(2,1)} async-done(((bf16[5,528,256]{2,1,0:T(8,128)(2,1)}), bf16[40,528,256]{2,1,0:T(8,128)(2,1)}) %all-gather.3.cloned.1.call-update) | async-done | bytes 10813456 | tf_op jit(solution)/shard_map/all_gather | solution.py:87
  275.2 3.8 compare_reduce_fusion.1
  279.1 0.1 copy.33
  279.2 0.1 ge.24
  279.2 0.1 copy.34
  279.3 0.1 le.27
  279.4 0.7 pad_add_fusion.meta_ref
  280.1 110.2 %shard_map.55 = bf16[512,512]{1,0:T(8,128)(2,1)} custom-call(s32[41]{0:T(128)} %pad_add_fusion.meta_ref, bf16[512,512]{1,0:T(8,128)(2,1)} %bitcast.46, f32[512,1]{1,0:T(8,128)} %copy.39.qseg_ref, bf16[8,5,528,256]{3,2,1,0:T(8,128)(2,1)} %bitcast.51), custom_call_target="tpu_custom_call" | custom-call | flops 21474836480 | bytes 11862016 | tf_op jit(solution)/shard_map/pallas_call | solution.py:180
  (13 shorter events, 0.2 us)
Async XLA Ops:
  6.5 43.1 %copy-start = (bf16[1024,512]{1,0:T(8,128)(2,1)S(1)}, bf16[1024,512]{1,0:T(8,128)(2,1)}, u32[]{:S(2)}) copy-start(bf16[1024,512]{1,0:T(8,128)(2,1)} %param.5) | copy-start | bytes 3145732
  9.1 7.5 %copy-start.3 = (s32[512]{0:T(512)S(1)}, s32[512]{0:T(512)}, u32[]{:S(2)}) copy-start(s32[512]{0:T(512)} %param.9) | copy-start | bytes 6148
  9.1 7.7 %copy-start.2 = (s32[8,8]{1,0:T(8,128)S(1)}, s32[8,8]{1,0:T(8,128)}, u32[]{:S(2)}) copy-start(s32[8,8]{1,0:T(8,128)} %param.7) | copy-start | bytes 772
  11.5 12.3 %all-to-all-start = ((bf16[8,1,128,256]{3,2,1,0:T(8,128)(2,1)}), bf16[8,1,128,256]{3,2,1,0:T(8,128)(2,1)S(1)}, u32[]{:S(2)}, u32[]{:S(2)}) async-start(bf16[8,1,128,256]{3,2,1,0:T(8,128)(2,1)} %copy.30), calls=%async_computation | async-start | bytes 1048576 | tf_op jit(solution)/shard_map/all_to_all | solution.py:60
  16.7 258.5 %all-gather.3.cloned.1.call-start = ((), (), s32[]{:S(2)}) async-start(), calls=%async_computation.2 | async-start | bytes 12165120 | tf_op jit(solution)/shard_map/all_gather | solution.py:87
  24.4 12.2 %collective-permute-start = (bf16[528,256]{1,0:T(8,128)(2,1)S(1)}, bf16[528,256]{1,0:T(8,128)(2,1)S(1)}, u32[]{:S(2)}, u32[]{:S(2)}) collective-permute-start(bf16[528,256]{1,0:T(8,128)(2,1)S(1)} %maximum_maximum_fusion), channel_id=1, source_target_pairs={{0,8},{8,16},{16,24},{24,32},{32,40},{40,48},{48,56},{56,64},{64,7... | collective-permute-start | bytes 811016 | tf_op jit(solution)/shard_map/ppermute | solution.py:14
  29.6 10.1 %collective-permute-start.1 = (bf16[528,256]{1,0:T(8,128)(2,1)S(1)}, bf16[528,256]{1,0:T(8,128)(2,1)S(1)}, u32[]{:S(2)}, u32[]{:S(2)}) collective-permute-start(bf16[528,256]{1,0:T(8,128)(2,1)S(1)} %maximum_maximum_fusion), channel_id=1, source_target_pairs={{0,16},{8,24},{16,32},{24,40},{32,48},{40,56},{48,64},{56,72},{64,... | collective-permute-start | bytes 811016 | tf_op jit(solution)/shard_map/ppermute | solution.py:14
  32.7 12.5 %collective-permute-start.2 = (bf16[528,256]{1,0:T(8,128)(2,1)S(1)}, bf16[528,256]{1,0:T(8,128)(2,1)S(1)}, u32[]{:S(2)}, u32[]{:S(2)}) collective-permute-start(bf16[528,256]{1,0:T(8,128)(2,1)S(1)} %maximum_maximum_fusion), channel_id=1, source_target_pairs={{0,24},{8,32},{16,40},{24,48},{32,56},{40,64},{48,72},{56,80},{64,... | collective-permute-start | bytes 811016 | tf_op jit(solution)/shard_map/ppermute | solution.py:14
  34.6 13.9 %collective-permute-start.3 = (bf16[528,256]{1,0:T(8,128)(2,1)S(1)}, bf16[528,256]{1,0:T(8,128)(2,1)S(1)}, u32[]{:S(2)}, u32[]{:S(2)}) collective-permute-start(bf16[528,256]{1,0:T(8,128)(2,1)S(1)} %maximum_maximum_fusion), channel_id=1, source_target_pairs={{0,32},{8,40},{16,48},{24,56},{32,64},{40,72},{48,80},{56,88},{64,... | collective-permute-start | bytes 811016 | tf_op jit(solution)/shard_map/ppermute | solution.py:14
  48.5 1.1 copy-start.1
  51.7 34.5 %all-to-all-start.1 = ((bf16[8,1,128,512]{3,2,1,0:T(8,128)(2,1)}), bf16[8,1,128,512]{3,2,1,0:T(8,128)(2,1)S(1)}, u32[]{:S(2)}, u32[]{:S(2)}) async-start(bf16[8,1,128,512]{3,2,1,0:T(8,128)(2,1)} %copy.36), calls=%async_computation.1 | async-start | bytes 2097152 | tf_op jit(solution)/shard_map/all_to_all | solution.py:59
Sparse Core Ops, SparseCore 0:
  49.7 225.4 all-gather.2
